TPU v7x, 256 devices: a whole 4x4x8 slice. The times are simulated.
256 devices in a mesh: seq: 32 (over y, x, z_lo), tp: 8 (over z_hi, core).
Axes of the slice: x: 4, y: 4, z: 8 (z_hi: 4, z_lo: 2; z = z_hi * 2 + z_lo), core: 2. Of those that a mesh axis runs over, the one named last changes fastest.
Arguments:
- tokens: bfloat16 [32768, 2048], P('seq'), may hold values from -20 to 20
- w_query: bfloat16 [2048, 2048], P(None, 'tp'), may hold values from -0.15467961 to 0.15467961
- w_kv: bfloat16 [2048, 512], replicated, may hold values from -0.110485435 to 0.110485435
- w_out: bfloat16 [2048, 2048], P('tp'), may hold values from -6 to 6
- seg_start: int32 [32768], P('seq'), may hold values from 0 to 32752, as said below
- page_owner: int32 [2048], replicated, may hold values from 0 to 31, as said below
- page_slot: int32 [2048], replicated, may hold values from 0 to 127, as said below
Outputs:
- layer_out: bfloat16 [32768, 2048], P('seq', 'tp')
- kv_cache: bfloat16 [65536, 512], P('seq', 'tp')
Inputs may be any that keep to these rules, and one draw needn't show every extreme that they name: seg_start[t] is the first position of the prompt that holds token t: it never falls along the stream, is a multiple of 16, is at most t, and equals t at each prompt's first token; the last page begins a prompt. `page_owner`: among the 64 pages of one stream block no owner is named more than 4 times; one owner is named exactly 4 times by the pages of every block. `page_slot`: pages with the same owner have distinct slots.
All inputs are finite; a program needn't handle non-finite values.
Results may differ from a plain program's by a relative error of at most 0.015.
Values may be sent and summed in bfloat16 or wider, within the bound.
No kernel may reach another device: no remote copies, remote signals or barrier semaphores. Data moves between devices by JAX's collectives and lax.ppermute only.
A program may use at most 64 MiB of HBM per device.

v0:
```python
import jax
import jax.numpy as jnp
from jax import lax
from jax.sharding import PartitionSpec as P

H = 32
KVH = 4
HD = 64
WINDOW = 2048
PAGE = 16


masked_value = -1e30


def passed_along(value, axis, steps):
    count = lax.axis_size(axis)
    leading, last = (max(0, -steps), min(count, count - steps))
    return lax.ppermute(value, axis, [(source, source + steps) for source in range(leading, last)])


def attend_band(query_block, band_block, positions_q, positions_k, starts):
    keys_block = band_block[:, :, 0, :]
    values_block = band_block[:, :, 1, :]
    head_size = query_block.shape[-1]
    scores = jnp.einsum(
        "qkgd,ckd->kgqc", query_block, keys_block, preferred_element_type=jnp.float32
    ) * head_size ** (-0.5)
    lower_bound = jnp.maximum(starts, positions_q - WINDOW + 1)
    visible = (positions_k[None, :] >= lower_bound[:, None]) & (
        positions_k[None, :] <= positions_q[:, None]
    )
    scores = jnp.where(visible, scores, masked_value)
    largest = jnp.max(scores, axis=-1, keepdims=True)
    powered = jnp.exp(scores - largest)
    row_total = jnp.sum(powered, axis=-1, keepdims=True)
    weights = powered.astype(jnp.bfloat16)
    result = (
        jnp.einsum("kgqc,ckd->kgqd", weights, values_block, preferred_element_type=jnp.float32)
        / row_total
    )
    return jnp.transpose(result, (2, 0, 1, 3)).astype(jnp.bfloat16)


def body(tokens, w_query, w_kv, w_out, seg_start, page_owner, page_slot):
    seq_index = lax.axis_index("seq")
    tp_index = lax.axis_index("tp")
    seq_count = lax.axis_size("seq")
    tp_count = lax.axis_size("tp")
    tok_rows = tokens.shape[0]
    group_size = H // KVH
    heads_dev = H // tp_count
    kv_heads_dev = max(1, heads_dev // group_size)
    kv_width = kv_heads_dev * 2 * HD
    cache_width = KVH * 2 * HD // tp_count
    first_col = tp_index * heads_dev // group_size * 2 * HD
    queries = jnp.dot(tokens, w_query, preferred_element_type=jnp.float32).astype(jnp.bfloat16)
    w_local = lax.dynamic_slice_in_dim(w_kv, first_col, kv_width, 1)
    key_value = jnp.dot(tokens, w_local, preferred_element_type=jnp.float32).astype(jnp.bfloat16)
    own_cols = lax.dynamic_slice_in_dim(
        key_value, tp_index * cache_width - first_col, cache_width, 1
    )
    pages_dev = tok_rows // PAGE
    slots_per = max(2, 2 * pages_dev // seq_count)
    cache_slots = seq_count * slots_per
    owners_all = page_owner.reshape(seq_count, pages_dev)
    owner_hot = (
        owners_all[:, :, None] == jnp.arange(seq_count, dtype=jnp.int32)[None, None, :]
    ).astype(jnp.int32)
    local_rank = jnp.sum((jnp.cumsum(owner_hot, axis=1) - owner_hot) * owner_hot, axis=2)
    column_of = jnp.arange(seq_count, dtype=jnp.int32)[:, None] * slots_per + local_rank
    own_owner = lax.dynamic_index_in_dim(owners_all, seq_index, 0, keepdims=False)
    own_rank = lax.dynamic_index_in_dim(local_rank, seq_index, 0, keepdims=False)
    destination = own_owner * slots_per + own_rank
    send_table = (jnp.arange(cache_slots, dtype=jnp.int32)[:, None] == destination[None, :]).astype(
        jnp.bfloat16
    )
    page_rows = own_cols.reshape(pages_dev, PAGE * cache_width)
    outgoing_pages = jnp.dot(send_table, page_rows, preferred_element_type=jnp.float32).astype(
        jnp.bfloat16
    )
    outgoing_pages = outgoing_pages.reshape(seq_count, slots_per, PAGE * cache_width)
    arrived = lax.all_to_all(outgoing_pages, "seq", split_axis=0, concat_axis=0, tiled=True)
    owned_here = page_owner == seq_index
    place_table = (
        (page_slot[None, :] == jnp.arange(cache_slots, dtype=jnp.int32)[:, None])
        & owned_here[None, :]
    ).astype(jnp.bfloat16)
    pick_table = (
        column_of.reshape(-1)[:, None] == jnp.arange(cache_slots, dtype=jnp.int32)[None, :]
    ).astype(jnp.bfloat16)
    route_table = jnp.dot(place_table, pick_table, preferred_element_type=jnp.float32).astype(
        jnp.bfloat16
    )
    cache_local = jnp.dot(
        route_table,
        arrived.reshape(cache_slots, PAGE * cache_width),
        preferred_element_type=jnp.float32,
    )
    kv_cache = cache_local.astype(jnp.bfloat16).reshape(cache_slots * PAGE, cache_width)
    blocks_back = WINDOW // tok_rows
    pieces = []
    for distance in range(blocks_back, 0, -1):
        pieces.append(passed_along(key_value, "seq", distance))
    behind = jnp.concatenate(pieces, axis=0)
    band_all = jnp.concatenate([behind, key_value], axis=0).reshape(-1, kv_heads_dev, 2, HD)
    query_heads = queries.reshape(tok_rows, kv_heads_dev, heads_dev // kv_heads_dev, HD)
    block_rows = min(256, tok_rows)
    base_position = seq_index * tok_rows

    def one_block(block_idx):
        first_row = block_idx * block_rows
        query_block = lax.dynamic_slice_in_dim(query_heads, first_row, block_rows, 0)
        band_block = lax.dynamic_slice_in_dim(band_all, first_row, WINDOW + block_rows, 0)
        starts = lax.dynamic_slice_in_dim(seg_start, first_row, block_rows, 0)
        positions_q = base_position + first_row + jnp.arange(block_rows, dtype=jnp.int32)
        positions_k = (
            base_position + first_row - WINDOW + jnp.arange(WINDOW + block_rows, dtype=jnp.int32)
        )
        return attend_band(query_block, band_block, positions_q, positions_k, starts)

    attended = lax.map(one_block, jnp.arange(tok_rows // block_rows, dtype=jnp.int32))
    attended = attended.reshape(tok_rows, heads_dev * HD)
    projected = jnp.dot(attended, w_out, preferred_element_type=jnp.float32)
    summed = lax.psum(projected.astype(jnp.bfloat16), "tp").astype(jnp.float32)
    width_dev = summed.shape[1] // tp_count
    layer_out = lax.dynamic_slice_in_dim(summed, tp_index * width_dev, width_dev, 1).astype(
        jnp.bfloat16
    )
    return (layer_out, kv_cache)


def solution(mesh):
    return jax.shard_map(
        body,
        mesh=mesh,
        in_specs=(P("seq", None), P(None, "tp"), P(), P("tp", None), P("seq"), P(), P()),
        out_specs=(P("seq", "tp"), P("seq", "tp")),
        check_vma=False,
    )
```

profile of v0, /device:TPU:65, one launch (start us, length us, event | category | flops | bytes accessed | tf_op | source)
XLA Modules:
  0.0 213.9 jit_solution(16457602136221309663)
XLA Ops:
  7.2 1.5 copy-done
  8.8 3.7 %convolution_convert_fusion.4 = bf16[128,1024]{1,0:T(8,128)(2,1)S(1)} fusion(bf16[1024,2048]{1,0:T(8,128)(2,1)} %param.9, bf16[2048,512]{1,0:T(8,128)(2,1)S(1)} %copy-done, s32[]{:T(128)S(6)} %select_n.52), kind=kOutput, calls=%fused_computation.32 | convolution fusion | flops 537001984 | bytes 4980740 | tf_op jit(solution)/shard_map/dot_general | solution.py:59
  12.5 3.6 %collective-permute-start.1 = (bf16[1024,128]{0,1:T(8,128)(2,1)S(1)}, bf16[1024,128]{0,1:T(8,128)(2,1)S(1)}, u32[]{:S(2)}, u32[]{:S(2)}) collective-permute-start(bf16[1024,128]{0,1:T(8,128)(2,1)S(1)} %bitcast.95), channel_id=1, source_target_pairs={{0,8},{8,16},{16,24},{24,32},{32,40},{40,48},{48,56},{56,64},{64,7... | collective-permute-start | bytes 786440 | tf_op jit(solution)/shard_map/ppermute | solution.py:19
  16.1 3.1 %collective-permute-start = (bf16[1024,128]{0,1:T(8,128)(2,1)S(1)}, bf16[1024,128]{0,1:T(8,128)(2,1)S(1)}, u32[]{:S(2)}, u32[]{:S(2)}) collective-permute-start(bf16[1024,128]{0,1:T(8,128)(2,1)S(1)} %bitcast.96), channel_id=1, source_target_pairs={{0,16},{8,24},{16,32},{24,40},{32,48},{40,56},{48,64},{56,72},{64,... | collective-permute-start | bytes 786440 | tf_op jit(solution)/shard_map/ppermute | solution.py:19
  19.2 4.6 %convolution_convert_fusion.1 = bf16[1024,256]{0,1:T(8,128)(2,1)} fusion(bf16[1024,2048]{1,0:T(8,128)(2,1)} %param.9, bf16[2048,256]{1,0:T(8,128)(2,1)} %param.10), kind=kOutput, calls=%fused_computation.29 | convolution fusion | flops 1074003968 | bytes 5767168 | tf_op jit(solution)/shard_map/dot_general | solution.py:57
  23.8 4.3 %collective-permute-done = bf16[1024,128]{0,1:T(8,128)(2,1)S(1)} collective-permute-done((bf16[1024,128]{0,1:T(8,128)(2,1)S(1)}, bf16[1024,128]{0,1:T(8,128)(2,1)S(1)}, u32[]{:S(2)}, u32[]{:S(2)}) %collective-permute-start) | collective-permute-done | bytes 262176 | tf_op jit(solution)/shard_map/ppermute | solution.py:19
  28.1 0.9 pad_maximum_fusion
  29.1 47.1 %while.15 = (s32[]{:T(128)}, bf16[4,256,1,4,64]{1,4,3,2,0:T(8,128)(2,1)}, s32[4]{0:T(128)S(1)}, s32[]{:T(128)}, s32[1024]{0:T(1024)}, /*index=5*/bf16[3072,1,2,6...) while((s32[]{:T(128)}, ...), condition=%wide.region_3.4_spmd, body=%wide.region_0.0_spmd.sunk | while | flops 631833600 | bytes 31567140 | solution.py:122
  29.1 0.6 dynamic_slice.80
  30.3 0.8 add_maximum_fusion.2
  31.1 1.1 compare_and_fusion.2
  32.2 2.6 %fusion.55 = (f32[4,256]{1,0:T(4,128)S(1)}, f32[2304,256,4]{1,0,2:T(8,128)S(1)}) fusion(pred[256,2304]{0,1:T(8,128)(4,1)S(1)} %compare_and_fusion.2, bf16[1024,1,4,64]{0,3,2,1:T(8,128)(2,1)} %get-tuple-element.277, s32[]{:T(128)S(6)} %select_n.82, bf16[3072,1,2,64]{0,3,2,1:T(8,128)(2,1)} %get-tuple-element.276, s32[]{:T(128)S(6)} %select_n.83), kind=kOutput, calls=%fused_computation.4.clone.1 | convolution fusion | flops 309066752 | bytes 10457096 | tf_op jit(solution)/shard_map/while/body/eval_jaxpr/qkgd,ckd->kgqc/dot_general | solution.py:26
  34.8 2.0 fusion.56
  36.8 4.1 %fusion.57 = bf16[4,256,1,4,64]{1,4,3,2,0:T(8,128)(2,1)} fusion(bf16[4,256,1,4,64]{1,4,3,2,0:T(8,128)(2,1)} %get-tuple-element.258, s32[]{:T(128)S(6)} %copy.40, f32[2304,256,4]{1,0,2:T(8,128)S(1)} %get-tuple-element.241, f32[4,256]{1,0:T(4,128)S(1)} %get-tuple-element.242, pred[256,2304]{0,1:T(8,128)(4,1)S(1)} %compare_and_fusion.2, ...), kind=kOutput, calls=%fused_computation.12.clone.1 | convolution fusion | flops 311558144 | bytes 10461196 | tf_op jit(solution)/shard_map/while/body/eval_jaxpr/kgqc,ckd->kgqd/dot_general | solution.py:39
  40.8 0.6 dynamic_slice.80
  42.1 0.8 add_maximum_fusion.2
  42.9 1.1 compare_and_fusion.2
  43.9 2.6 %fusion.55 = (f32[4,256]{1,0:T(4,128)S(1)}, f32[2304,256,4]{1,0,2:T(8,128)S(1)}) fusion(pred[256,2304]{0,1:T(8,128)(4,1)S(1)} %compare_and_fusion.2, bf16[1024,1,4,64]{0,3,2,1:T(8,128)(2,1)} %get-tuple-element.277, s32[]{:T(128)S(6)} %select_n.82, bf16[3072,1,2,64]{0,3,2,1:T(8,128)(2,1)} %get-tuple-element.276, s32[]{:T(128)S(6)} %select_n.83), kind=kOutput, calls=%fused_computation.4.clone.1 | convolution fusion | flops 309066752 | bytes 10457096 | tf_op jit(solution)/shard_map/while/body/eval_jaxpr/qkgd,ckd->kgqc/dot_general | solution.py:26
  46.6 2.0 fusion.56
  48.6 4.1 %fusion.57 = bf16[4,256,1,4,64]{1,4,3,2,0:T(8,128)(2,1)} fusion(bf16[4,256,1,4,64]{1,4,3,2,0:T(8,128)(2,1)} %get-tuple-element.258, s32[]{:T(128)S(6)} %copy.40, f32[2304,256,4]{1,0,2:T(8,128)S(1)} %get-tuple-element.241, f32[4,256]{1,0:T(4,128)S(1)} %get-tuple-element.242, pred[256,2304]{0,1:T(8,128)(4,1)S(1)} %compare_and_fusion.2, ...), kind=kOutput, calls=%fused_computation.12.clone.1 | convolution fusion | flops 311558144 | bytes 10461196 | tf_op jit(solution)/shard_map/while/body/eval_jaxpr/kgqc,ckd->kgqd/dot_general | solution.py:39
  52.6 0.6 dynamic_slice.80
  53.9 0.8 add_maximum_fusion.2
  54.6 1.1 compare_and_fusion.2
  55.7 2.6 %fusion.55 = (f32[4,256]{1,0:T(4,128)S(1)}, f32[2304,256,4]{1,0,2:T(8,128)S(1)}) fusion(pred[256,2304]{0,1:T(8,128)(4,1)S(1)} %compare_and_fusion.2, bf16[1024,1,4,64]{0,3,2,1:T(8,128)(2,1)} %get-tuple-element.277, s32[]{:T(128)S(6)} %select_n.82, bf16[3072,1,2,64]{0,3,2,1:T(8,128)(2,1)} %get-tuple-element.276, s32[]{:T(128)S(6)} %select_n.83), kind=kOutput, calls=%fused_computation.4.clone.1 | convolution fusion | flops 309066752 | bytes 10457096 | tf_op jit(solution)/shard_map/while/body/eval_jaxpr/qkgd,ckd->kgqc/dot_general | solution.py:26
  58.3 2.0 fusion.56
  60.3 4.1 %fusion.57 = bf16[4,256,1,4,64]{1,4,3,2,0:T(8,128)(2,1)} fusion(bf16[4,256,1,4,64]{1,4,3,2,0:T(8,128)(2,1)} %get-tuple-element.258, s32[]{:T(128)S(6)} %copy.40, f32[2304,256,4]{1,0,2:T(8,128)S(1)} %get-tuple-element.241, f32[4,256]{1,0:T(4,128)S(1)} %get-tuple-element.242, pred[256,2304]{0,1:T(8,128)(4,1)S(1)} %compare_and_fusion.2, ...), kind=kOutput, calls=%fused_computation.12.clone.1 | convolution fusion | flops 311558144 | bytes 10461196 | tf_op jit(solution)/shard_map/while/body/eval_jaxpr/kgqc,ckd->kgqd/dot_general | solution.py:39
  64.4 0.6 dynamic_slice.80
  65.6 0.8 add_maximum_fusion.2
  66.4 1.1 compare_and_fusion.2
  67.5 2.6 %fusion.55 = (f32[4,256]{1,0:T(4,128)S(1)}, f32[2304,256,4]{1,0,2:T(8,128)S(1)}) fusion(pred[256,2304]{0,1:T(8,128)(4,1)S(1)} %compare_and_fusion.2, bf16[1024,1,4,64]{0,3,2,1:T(8,128)(2,1)} %get-tuple-element.277, s32[]{:T(128)S(6)} %select_n.82, bf16[3072,1,2,64]{0,3,2,1:T(8,128)(2,1)} %get-tuple-element.276, s32[]{:T(128)S(6)} %select_n.83), kind=kOutput, calls=%fused_computation.4.clone.1 | convolution fusion | flops 309066752 | bytes 10457096 | tf_op jit(solution)/shard_map/while/body/eval_jaxpr/qkgd,ckd->kgqc/dot_general | solution.py:26
  70.1 2.0 fusion.56
  72.1 4.1 %fusion.57 = bf16[4,256,1,4,64]{1,4,3,2,0:T(8,128)(2,1)} fusion(bf16[4,256,1,4,64]{1,4,3,2,0:T(8,128)(2,1)} %get-tuple-element.258, s32[]{:T(128)S(6)} %copy.40, f32[2304,256,4]{1,0,2:T(8,128)S(1)} %get-tuple-element.241, f32[4,256]{1,0:T(4,128)S(1)} %get-tuple-element.242, pred[256,2304]{0,1:T(8,128)(4,1)S(1)} %compare_and_fusion.2, ...), kind=kOutput, calls=%fused_computation.12.clone.1 | convolution fusion | flops 311558144 | bytes 10461196 | tf_op jit(solution)/shard_map/while/body/eval_jaxpr/kgqc,ckd->kgqd/dot_general | solution.py:39
  76.2 1.4 copy.29
  77.6 0.1 copy.36
  77.7 3.3 %convolution_convert_fusion = bf16[1024,2048]{1,0:T(8,128)(2,1)} fusion(bf16[1024,256]{0,1:T(8,128)(2,1)S(1)} %bitcast.93, bf16[256,2048]{1,0:T(8,128)(2,1)S(1)} %copy-done.1), kind=kOutput, calls=%fused_computation.25 | convolution fusion | flops 1075838976 | bytes 5767168 | tf_op jit(solution)/shard_map/dot_general | solution.py:124
  81.2 0.2 copy.33
  81.4 0.2 reshape.132
  81.6 1.7 select_reduce_fusion
  83.3 0.2 add_reduce_fusion
  83.5 0.2 convolution_convert_fusion.3
  83.7 0.8 reshape.133
  84.6 8.0 %all-to-all-start = ((bf16[32,4,1024]{2,1,0:T(4,128)(2,1)}), bf16[32,4,1024]{2,1,0:T(4,128)(2,1)S(1)}, u32[]{:S(2)}, u32[]{:S(2)}) async-start(bf16[32,4,1024]{2,1,0:T(4,128)(2,1)} %reshape.133), calls=%async_computation | async-start | bytes 524288 | tf_op jit(solution)/shard_map/all_to_all | solution.py:83
  92.8 8.5 %all-to-all-done = bf16[32,4,1024]{2,1,0:T(4,128)(2,1)S(1)} async-done(((bf16[32,4,1024]{2,1,0:T(4,128)(2,1)}), bf16[32,4,1024]{2,1,0:T(4,128)(2,1)S(1)}, u32[]{:S(2)}, u32[]{:S(2)}) %all-to-all-start) | async-done | bytes 262176 | tf_op jit(solution)/shard_map/all_to_all | solution.py:83
  101.4 0.7 convolution_convert_fusion.2
  102.1 0.3 reshape.135
  102.5 0.9 copy.34
  103.4 101.8 %all-reduce.2.cloned.1.call-done = bf16[1024,2048]{1,0:T(8,128)(2,1)} async-done(((bf16[1024,2048]{1,0:T(8,128)(2,1)}), bf16[1024,2048]{1,0:T(8,128)(2,1)}) %all-reduce.2.cloned.1.call-update) | async-done | bytes 4194320 | tf_op jit(solution)/shard_map/psum | solution.py:125
  205.2 1.9 convert_convert_fusion
  (25 shorter events, 0.5 us)
Async XLA Ops:
  7.2 1.6 copy-start
  7.2 198.0 %all-reduce.2.cloned.1.call-start = ((), (), s32[]{:S(2)}) async-start(), calls=%async_computation.1 | async-start | bytes 8388608 | tf_op jit(solution)/shard_map/psum | solution.py:125
  12.5 11.3 %collective-permute-start.1 = (bf16[1024,128]{0,1:T(8,128)(2,1)S(1)}, bf16[1024,128]{0,1:T(8,128)(2,1)S(1)}, u32[]{:S(2)}, u32[]{:S(2)}) collective-permute-start(bf16[1024,128]{0,1:T(8,128)(2,1)S(1)} %bitcast.95), channel_id=1, source_target_pairs={{0,8},{8,16},{16,24},{24,32},{32,40},{40,48},{48,56},{56,64},{64,7... | collective-permute-start | bytes 786440 | tf_op jit(solution)/shard_map/ppermute | solution.py:19
  16.1 12.1 %collective-permute-start = (bf16[1024,128]{0,1:T(8,128)(2,1)S(1)}, bf16[1024,128]{0,1:T(8,128)(2,1)S(1)}, u32[]{:S(2)}, u32[]{:S(2)}) collective-permute-start(bf16[1024,128]{0,1:T(8,128)(2,1)S(1)} %bitcast.96), channel_id=1, source_target_pairs={{0,16},{8,24},{16,32},{24,40},{32,48},{40,56},{48,64},{56,72},{64,... | collective-permute-start | bytes 786440 | tf_op jit(solution)/shard_map/ppermute | solution.py:19
  29.1 48.6 %copy-start.1 = (bf16[256,2048]{1,0:T(8,128)(2,1)S(1)}, bf16[256,2048]{1,0:T(8,128)(2,1)}, u32[]{:S(2)}) copy-start(bf16[256,2048]{1,0:T(8,128)(2,1)} %param.12) | copy-start | bytes 3145732
  77.7 3.3 %copy-start.2 = (s32[2048]{0:T(1024)S(1)}, s32[2048]{0:T(1024)}, u32[]{:S(2)}) copy-start(s32[2048]{0:T(1024)} %param.14) | copy-start | bytes 24580
  81.0 20.4 %copy-start.3 = (s32[2048]{0:T(1024)S(1)}, s32[2048]{0:T(1024)}, u32[]{:S(2)}) copy-start(s32[2048]{0:T(1024)} %param.15) | copy-start | bytes 24580
  84.6 16.8 %all-to-all-start = ((bf16[32,4,1024]{2,1,0:T(4,128)(2,1)}), bf16[32,4,1024]{2,1,0:T(4,128)(2,1)S(1)}, u32[]{:S(2)}, u32[]{:S(2)}) async-start(bf16[32,4,1024]{2,1,0:T(4,128)(2,1)} %reshape.133), calls=%async_computation | async-start | bytes 524288 | tf_op jit(solution)/shard_map/all_to_all | solution.py:83
Sparse Core Ops, SparseCore 0:
  81.2 124.0 all-reduce.1
where the time goes:
time: 215 us; the launch traced here: 214 us
  waiting for transfers between devices  115 us (53%)
  matrix products  39.2 us (18%)
  other arithmetic  20.2 us (9%)
  starting transfers between devices  14.7 us (7%)
  between operations  14.2 us (7%)
  local copies, waits for them, and re-layouts  8.25 us (4%)
  loops' own time  2.64 us (1%)
    psum x1, waiting for transfers between devices, body(): summed = lax.psum(projected.astype(jnp.bfloat16), 'tp').astype(jnp.float32)  102 us
    dot_general x4, matrix products, attend_band(): jnp.einsum('kgqc,ckd->kgqd', weights, values_block, preferred_element_typ...  16.3 us
    dot_general x4, matrix products, attend_band(): jnp.einsum('qkgd,ckd->kgqc', query_block, keys_block, preferred_element_t...  10.4 us
    all_to_all x1, waiting for transfers between devices, body(): lax.all_to_all(outgoing_pages, 'seq', split_axis=0, concat_axis=0, tiled=...  8.51 us
    all_to_all x1, starting transfers between devices, body(): lax.all_to_all(outgoing_pages, 'seq', split_axis=0, concat_axis=0, tiled=...  8.02 us
    reduce_sum x4, other arithmetic, attend_band(): row_total = jnp.sum(powered, axis=-1, keepdims=True)  7.98 us
    ppermute x2, starting transfers between devices, passed_along(): lax.ppermute(value, axis, [(source, source + steps) for source in range(l...  6.68 us
    dot_general x1, matrix products, body(): jnp.dot(tokens, w_query, preferred_element_type=jnp.float32)  4.58 us
  transfers between devices with their start and end apart: 4, of which 3 were waited for; matrix products, arithmetic and copies ran while one was open for 5% of the time, Pallas kernels for 0%

commit v1 on v0

--- a/solution.py
+++ b/solution.py
@@ -119,14 +119,14 @@
         )
         return attend_band(query_block, band_block, positions_q, positions_k, starts)
 
-    attended = lax.map(one_block, jnp.arange(tok_rows // block_rows, dtype=jnp.int32))
-    attended = attended.reshape(tok_rows, heads_dev * HD)
-    projected = jnp.dot(attended, w_out, preferred_element_type=jnp.float32)
-    summed = lax.psum(projected.astype(jnp.bfloat16), "tp").astype(jnp.float32)
-    width_dev = summed.shape[1] // tp_count
-    layer_out = lax.dynamic_slice_in_dim(summed, tp_index * width_dev, width_dev, 1).astype(
-        jnp.bfloat16
-    )
+    out_blocks = []
+    for block_idx in range(tok_rows // block_rows):
+        attended = one_block(block_idx).reshape(block_rows, heads_dev * HD)
+        projected = jnp.dot(attended, w_out, preferred_element_type=jnp.float32)
+        out_blocks.append(
+            lax.psum_scatter(projected.astype(jnp.bfloat16), "tp", scatter_dimension=1, tiled=True)
+        )
+    layer_out = jnp.concatenate(out_blocks, axis=0)
     return (layer_out, kv_cache)
 
 

time: 215 us -> 213 us (level)
  waiting for transfers between devices: 115 us -> 124 us
  matrix products: 39.2 us -> 34.3 us
  loops' own time: 2.64 us -> 0 us
    reduce_scatter x0 -> x4, waiting for transfers between devices: none -> 115 us  [body(): lax.psum_scatter(projected.astype(jnp.bfloat16), 'tp', scatter_dimension=...]
    psum x1 -> x0, waiting for transfers between devices: 102 us -> none  [body(): summed = lax.psum(projected.astype(jnp.bfloat16), 'tp').astype(jnp.float32)]
    dot_general x4, matrix products: 16.3 us -> 9.71 us  [attend_band(): jnp.einsum('kgqc,ckd->kgqd', weights, values_block, preferred_element_typ...]
    ppermute x2, waiting for transfers between devices: 4.35 us -> 0.01 us  [passed_along(): lax.ppermute(value, axis, [(source, source + steps) for source in range(l...]
    another operation x1 -> x0, loops' own time: 2.64 us -> none  [body(): lax.map(one_block, jnp.arange(tok_rows // block_rows, dtype=jnp.int32))]
    dot_general x1 -> x4, matrix products: 3.28 us -> 5.86 us  [body(): projected = jnp.dot(attended, w_out, preferred_element_type=jnp.float32)]
    max x4 -> x1, other arithmetic: 3.06 us -> 0.85 us  [attend_band(): lower_bound = jnp.maximum(starts, positions_q - WINDOW + 1)]
    and x4, other arithmetic: 4.32 us -> 6.48 us  [attend_band(): (positions_k[None, :] >= lower_bound[:, None]) & (positions_k[None, :] <=...]
  transfers between devices with their start and end apart: 4 -> 7, of which waited for: 3 -> 4; matrix products, arithmetic and copies ran while one was open for 5% -> 21% of each run, Pallas kernels for 0% -> 0%
where the time goes in v1:
time: 213 us; the launch traced here: 212 us
  waiting for transfers between devices  124 us (58%)
  matrix products  34.3 us (16%)
  other arithmetic  19.3 us (9%)
  starting transfers between devices  14.2 us (7%)
  between operations  14.1 us (7%)
  local copies, waits for them, and re-layouts  6.36 us (3%)
    reduce_scatter x4, waiting for transfers between devices, body(): lax.psum_scatter(projected.astype(jnp.bfloat16), 'tp', scatter_dimension=...  115 us
    dot_general x4, matrix products, attend_band(): jnp.einsum('qkgd,ckd->kgqc', query_block, keys_block, preferred_element_t...  10.3 us
    dot_general x4, matrix products, attend_band(): jnp.einsum('kgqc,ckd->kgqd', weights, values_block, preferred_element_typ...  9.71 us
    all_to_all x1, waiting for transfers between devices, body(): lax.all_to_all(outgoing_pages, 'seq', split_axis=0, concat_axis=0, tiled=...  8.63 us
    reduce_sum x4, other arithmetic, attend_band(): row_total = jnp.sum(powered, axis=-1, keepdims=True)  7.98 us
    all_to_all x1, starting transfers between devices, body(): lax.all_to_all(outgoing_pages, 'seq', split_axis=0, concat_axis=0, tiled=...  6.94 us
    ppermute x2, starting transfers between devices, passed_along(): lax.ppermute(value, axis, [(source, source + steps) for source in range(l...  6.69 us
    and x4, other arithmetic, attend_band(): (positions_k[None, :] >= lower_bound[:, None]) & (positions_k[None, :] <=...  6.48 us
  transfers between devices with their start and end apart: 7, of which 4 were waited for; matrix products, arithmetic and copies ran while one was open for 21% of the time, Pallas kernels for 0%

profile of v1, /device:TPU:65, one launch (start us, length us, event | category | flops | bytes accessed | tf_op | source)
XLA Modules:
  0.0 212.0 jit_solution(7252337664588854691)
XLA Ops:
  7.2 1.5 copy-done
  8.8 3.7 %convolution_convert_fusion.7 = bf16[128,1024]{1,0:T(8,128)(2,1)S(1)} fusion(bf16[1024,2048]{1,0:T(8,128)(2,1)} %param.7, bf16[2048,512]{1,0:T(8,128)(2,1)S(1)} %copy-done, s32[]{:T(128)S(6)} %select_n.30), kind=kOutput, calls=%fused_computation.46 | convolution fusion | flops 537001984 | bytes 4980740 | tf_op jit(solution)/shard_map/dot_general | solution.py:59
  12.5 3.1 %collective-permute-start = (bf16[1024,128]{0,1:T(8,128)(2,1)S(1)}, bf16[1024,128]{0,1:T(8,128)(2,1)S(1)}, u32[]{:S(2)}, u32[]{:S(2)}) collective-permute-start(bf16[1024,128]{0,1:T(8,128)(2,1)S(1)} %bitcast.192), channel_id=1, source_target_pairs={{0,16},{8,24},{16,32},{24,40},{32,48},{40,56},{48,64},{56,72},{64,... | collective-permute-start | bytes 786440 | tf_op jit(solution)/shard_map/ppermute | solution.py:19
  15.6 3.6 %collective-permute-start.1 = (bf16[1024,128]{0,1:T(8,128)(2,1)S(1)}, bf16[1024,128]{0,1:T(8,128)(2,1)S(1)}, u32[]{:S(2)}, u32[]{:S(2)}) collective-permute-start(bf16[1024,128]{0,1:T(8,128)(2,1)S(1)} %bitcast.193), channel_id=1, source_target_pairs={{0,8},{8,16},{16,24},{24,32},{32,40},{40,48},{48,56},{56,64},{64,7... | collective-permute-start | bytes 786440 | tf_op jit(solution)/shard_map/ppermute | solution.py:19
  19.2 0.8 add_maximum_fusion.3
  20.1 1.1 compare_and_fusion.3
  21.3 1.8 compare_and_fusion.2
  23.1 1.8 compare_and_fusion.1
  24.8 1.8 compare_and_fusion
  26.6 3.8 %convolution_convert_fusion.4 = bf16[1024,256]{0,1:T(8,128)(2,1)S(1)} fusion(bf16[1024,2048]{1,0:T(8,128)(2,1)} %param.7, bf16[2048,256]{1,0:T(8,128)(2,1)} %param.8), kind=kOutput, calls=%fused_computation.43 | convolution fusion | flops 1074003968 | bytes 5767168 | tf_op jit(solution)/shard_map/dot_general | solution.py:57
  30.4 0.7 fusion.82
  31.2 1.3 fusion.81
  32.5 1.6 fusion.8
  34.1 2.0 fusion
  36.1 2.4 %fusion.53 = bf16[4,256,64]{1,2,0:T(8,128)(2,1)S(1)} fusion(f32[2304,256,4]{1,0,2:T(8,128)S(1)} %get-tuple-element.31, f32[4,256]{1,0:T(4,128)S(1)} %get-tuple-element.30, pred[256,2304]{0,1:T(8,128)(4,1)S(1)} %compare_and_fusion.3, bf16[2304,1,2,64]{0,3,2,1:T(8,128)(2,1)S(1)} %bitcast.202, f32[4,256]{1,0:T(4,128)S(1)} %fusion), kind=kOutput, calls=%fused_computation.55 | convolution fusion | flops 311558144 | bytes 10461184 | tf_op jit(solution)/shard_map/kgqc,ckd->kgqd/dot_general | solution.py:39
  38.5 1.5 convolution_convert_fusion.3
  40.0 0.2 reduce-scatter.7.cloned.1.call-start
  40.3 2.9 %fusion.9 = (f32[4,256]{1,0:T(4,128)S(1)}, f32[2304,256,4]{1,0,2:T(8,128)S(1)}) fusion(pred[256,2304]{0,1:T(8,128)(4,1)} %compare_and_fusion.2, bf16[256,4,64]{0,2,1:T(8,128)(2,1)} %bitcast.209, bf16[2304,1,2,64]{0,3,2,1:T(8,128)(2,1)} %bitcast.199), kind=kOutput, calls=%fused_computation.17 | convolution fusion | flops 309066752 | bytes 10457088 | tf_op jit(solution)/shard_map/qkgd,ckd->kgqc/dot_general | solution.py:26
  43.2 2.0 fusion.2
  45.2 2.4 %fusion.47 = bf16[4,256,64]{1,2,0:T(8,128)(2,1)S(1)} fusion(f32[2304,256,4]{1,0,2:T(8,128)S(1)} %get-tuple-element.29, f32[4,256]{1,0:T(4,128)S(1)} %get-tuple-element.28, pred[256,2304]{0,1:T(8,128)(4,1)S(1)} %copy-done.4, bf16[2304,1,2,64]{0,3,2,1:T(8,128)(2,1)S(1)} %bitcast.200, f32[4,256]{1,0:T(4,128)S(1)} %fusion.2), kind=kOutput, calls=%fused_computation.53 | convolution fusion | flops 311558144 | bytes 10461184 | tf_op jit(solution)/shard_map/kgqc,ckd->kgqd/dot_general | solution.py:39
  47.6 1.5 convolution_convert_fusion.2
  49.2 2.9 %fusion.10 = (f32[4,256]{1,0:T(4,128)S(1)}, f32[2304,256,4]{1,0,2:T(8,128)S(1)}) fusion(pred[256,2304]{0,1:T(8,128)(4,1)} %compare_and_fusion.1, bf16[256,4,64]{0,2,1:T(8,128)(2,1)} %bitcast.208, bf16[2304,1,2,64]{0,3,2,1:T(8,128)(2,1)} %bitcast.197), kind=kOutput, calls=%fused_computation.18 | convolution fusion | flops 309066752 | bytes 10457088 | tf_op jit(solution)/shard_map/qkgd,ckd->kgqc/dot_general | solution.py:26
  52.1 2.0 fusion.4
  54.1 2.4 %fusion.41 = bf16[4,256,64]{1,2,0:T(8,128)(2,1)S(1)} fusion(f32[2304,256,4]{1,0,2:T(8,128)S(1)} %get-tuple-element.27, f32[4,256]{1,0:T(4,128)S(1)} %get-tuple-element.26, pred[256,2304]{0,1:T(8,128)(4,1)S(1)} %copy-done.3, bf16[2304,1,2,64]{0,3,2,1:T(8,128)(2,1)S(1)} %bitcast.198, f32[4,256]{1,0:T(4,128)S(1)} %fusion.4), kind=kOutput, calls=%fused_computation.51 | convolution fusion | flops 311558144 | bytes 10461184 | tf_op jit(solution)/shard_map/kgqc,ckd->kgqd/dot_general | solution.py:39
  56.6 1.5 convolution_convert_fusion.1
  58.0 0.3 reduce-scatter.11.cloned.1.call-start
  58.3 2.9 %fusion.11 = (f32[4,256]{1,0:T(4,128)S(1)}, f32[2304,256,4]{1,0,2:T(8,128)S(1)}) fusion(pred[256,2304]{0,1:T(8,128)(4,1)} %compare_and_fusion, bf16[256,4,64]{0,2,1:T(8,128)(2,1)S(1)} %bitcast.207, bf16[2304,1,2,64]{0,3,2,1:T(8,128)(2,1)} %bitcast.195), kind=kOutput, calls=%fused_computation.19 | convolution fusion | flops 309066752 | bytes 10457088 | tf_op jit(solution)/shard_map/qkgd,ckd->kgqc/dot_general | solution.py:26
  61.2 2.0 fusion.6
  63.2 2.4 %fusion.35 = bf16[4,256,64]{1,2,0:T(8,128)(2,1)S(1)} fusion(f32[2304,256,4]{1,0,2:T(8,128)S(1)} %get-tuple-element.25, f32[4,256]{1,0:T(4,128)S(1)} %get-tuple-element.24, pred[256,2304]{0,1:T(8,128)(4,1)S(1)} %copy-done.2, bf16[2304,1,2,64]{0,3,2,1:T(8,128)(2,1)S(1)} %bitcast.196, f32[4,256]{1,0:T(4,128)S(1)} %fusion.6), kind=kOutput, calls=%fused_computation.49 | convolution fusion | flops 311558144 | bytes 10461184 | tf_op jit(solution)/shard_map/kgqc,ckd->kgqd/dot_general | solution.py:39
  65.7 1.4 convolution_convert_fusion
  67.2 0.2 copy.44
  67.4 0.2 reshape.239
  67.6 0.1 copy.41
  67.7 1.7 select_reduce_fusion
  69.4 0.2 add_reduce_fusion
  69.6 0.2 convolution_convert_fusion.6
  69.9 0.8 reshape.240
  70.7 6.9 %all-to-all-start = ((bf16[32,4,1024]{2,1,0:T(4,128)(2,1)}), bf16[32,4,1024]{2,1,0:T(4,128)(2,1)S(1)}, u32[]{:S(2)}, u32[]{:S(2)}) async-start(bf16[32,4,1024]{2,1,0:T(4,128)(2,1)} %reshape.240), calls=%async_computation.4 | async-start | bytes 524288 | tf_op jit(solution)/shard_map/all_to_all | solution.py:83
  77.7 0.1 broadcast_add_fusion
  77.8 0.1 add.194
  77.8 8.6 %all-to-all-done = bf16[32,4,1024]{2,1,0:T(4,128)(2,1)S(1)} async-done(((bf16[32,4,1024]{2,1,0:T(4,128)(2,1)}), bf16[32,4,1024]{2,1,0:T(4,128)(2,1)S(1)}, u32[]{:S(2)}, u32[]{:S(2)}) %all-to-all-start) | async-done | bytes 262176 | tf_op jit(solution)/shard_map/all_to_all | solution.py:83
  86.5 0.7 convolution_convert_fusion.5
  87.3 0.3 reshape.242
  87.6 0.9 copy.45
  88.5 34.1 %reduce-scatter.7.cloned.1.call-done = bf16[256,256]{1,0:T(8,128)(2,1)} async-done(((bf16[256,2048]{1,0:T(8,128)(2,1)}), bf16[256,256]{1,0:T(8,128)(2,1)}) %reduce-scatter.7.cloned.1.call-update) | async-done | bytes 131088 | tf_op jit(solution)/shard_map/reduce_scatter | solution.py:127
  122.6 40.7 %reduce-scatter.9.cloned.1.call-done = bf16[256,256]{1,0:T(8,128)(2,1)} async-done(((bf16[256,2048]{1,0:T(8,128)(2,1)}), bf16[256,256]{1,0:T(8,128)(2,1)}) %reduce-scatter.9.cloned.1.call-update) | async-done | bytes 131088 | tf_op jit(solution)/shard_map/reduce_scatter | solution.py:127
  163.2 40.3 %reduce-scatter.11.cloned.1.call-done = bf16[256,256]{1,0:T(8,128)(2,1)} async-done(((bf16[256,2048]{1,0:T(8,128)(2,1)}), bf16[256,256]{1,0:T(8,128)(2,1)}) %reduce-scatter.11.cloned.1.call-update) | async-done | bytes 131088 | tf_op jit(solution)/shard_map/reduce_scatter | solution.py:127
  203.5 1.9 pad_maximum_fusion.1
  (42 shorter events, 0.5 us)
Async XLA Ops:
  7.2 1.6 copy-start
  7.2 81.3 %reduce-scatter.5.cloned.1.call-start = ((), (), s32[]{:S(2)}) async-start(), calls=%async_computation.5 | async-start | bytes 1179648 | tf_op jit(solution)/shard_map/reduce_scatter | solution.py:127
  12.5 18.7 %collective-permute-start = (bf16[1024,128]{0,1:T(8,128)(2,1)S(1)}, bf16[1024,128]{0,1:T(8,128)(2,1)S(1)}, u32[]{:S(2)}, u32[]{:S(2)}) collective-permute-start(bf16[1024,128]{0,1:T(8,128)(2,1)S(1)} %bitcast.192), channel_id=1, source_target_pairs={{0,16},{8,24},{16,32},{24,40},{32,48},{40,56},{48,64},{56,72},{64,... | collective-permute-start | bytes 786440 | tf_op jit(solution)/shard_map/ppermute | solution.py:19
  15.6 15.5 %collective-permute-start.1 = (bf16[1024,128]{0,1:T(8,128)(2,1)S(1)}, bf16[1024,128]{0,1:T(8,128)(2,1)S(1)}, u32[]{:S(2)}, u32[]{:S(2)}) collective-permute-start(bf16[1024,128]{0,1:T(8,128)(2,1)S(1)} %bitcast.193), channel_id=1, source_target_pairs={{0,8},{8,16},{16,24},{24,32},{32,40},{40,48},{48,56},{56,64},{64,7... | collective-permute-start | bytes 786440 | tf_op jit(solution)/shard_map/ppermute | solution.py:19
  36.1 2.4 %copy-start.1 = (bf16[256,2048]{1,0:T(8,128)(2,1)S(1)}, bf16[256,2048]{1,0:T(8,128)(2,1)}, u32[]{:S(2)}) copy-start(bf16[256,2048]{1,0:T(8,128)(2,1)} %param.10) | copy-start | bytes 3145732
  40.0 82.6 %reduce-scatter.7.cloned.1.call-start = ((), (), s32[]{:S(2)}) async-start(), calls=%async_computation.6 | async-start | bytes 1179648 | tf_op jit(solution)/shard_map/reduce_scatter | solution.py:127
  40.2 2.9 %copy-start.4 = (pred[256,2304]{0,1:T(8,128)(4,1)S(1)}, pred[256,2304]{0,1:T(8,128)(4,1)}, u32[]{:S(2)}) copy-start(pred[256,2304]{0,1:T(8,128)(4,1)} %compare_and_fusion.2) | copy-start | bytes 1769476
  40.3 4.9 %copy-start.7 = (bf16[2304,128]{0,1:T(8,128)(2,1)S(1)}, bf16[2304,128]{0,1:T(8,128)(2,1)}, u32[]{:S(2)}) copy-start(bf16[2304,128]{0,1:T(8,128)(2,1)} %get-tuple-element.15) | copy-start | bytes 1769476
  49.1 114.1 %reduce-scatter.9.cloned.1.call-start = ((), (), s32[]{:S(2)}) async-start(), calls=%async_computation.7 | async-start | bytes 1179648 | tf_op jit(solution)/shard_map/reduce_scatter | solution.py:127
  49.2 2.9 %copy-start.3 = (pred[256,2304]{0,1:T(8,128)(4,1)S(1)}, pred[256,2304]{0,1:T(8,128)(4,1)}, u32[]{:S(2)}) copy-start(pred[256,2304]{0,1:T(8,128)(4,1)} %compare_and_fusion.1) | copy-start | bytes 1769476
  49.2 4.9 %copy-start.6 = (bf16[2304,128]{0,1:T(8,128)(2,1)S(1)}, bf16[2304,128]{0,1:T(8,128)(2,1)}, u32[]{:S(2)}) copy-start(bf16[2304,128]{0,1:T(8,128)(2,1)} %get-tuple-element.14) | copy-start | bytes 1769476
  58.0 145.5 %reduce-scatter.11.cloned.1.call-start = ((), (), s32[]{:S(2)}) async-start(), calls=%async_computation.8 | async-start | bytes 1179648 | tf_op jit(solution)/shard_map/reduce_scatter | solution.py:127
  58.3 2.9 %copy-start.2 = (pred[256,2304]{0,1:T(8,128)(4,1)S(1)}, pred[256,2304]{0,1:T(8,128)(4,1)}, u32[]{:S(2)}) copy-start(pred[256,2304]{0,1:T(8,128)(4,1)} %compare_and_fusion) | copy-start | bytes 1769476
  58.3 4.9 %copy-start.5 = (bf16[2304,128]{0,1:T(8,128)(2,1)S(1)}, bf16[2304,128]{0,1:T(8,128)(2,1)}, u32[]{:S(2)}) copy-start(bf16[2304,128]{0,1:T(8,128)(2,1)} %get-tuple-element.13) | copy-start | bytes 1769476
  63.2 4.3 %copy-start.8 = (s32[2048]{0:T(1024)S(1)}, s32[2048]{0:T(1024)}, u32[]{:S(2)}) copy-start(s32[2048]{0:T(1024)} %param.12) | copy-start | bytes 24580
  63.2 23.3 %copy-start.9 = (s32[2048]{0:T(1024)S(1)}, s32[2048]{0:T(1024)}, u32[]{:S(2)}) copy-start(s32[2048]{0:T(1024)} %param.13) | copy-start | bytes 24580
  70.7 15.8 %all-to-all-start = ((bf16[32,4,1024]{2,1,0:T(4,128)(2,1)}), bf16[32,4,1024]{2,1,0:T(4,128)(2,1)S(1)}, u32[]{:S(2)}, u32[]{:S(2)}) async-start(bf16[32,4,1024]{2,1,0:T(4,128)(2,1)} %reshape.240), calls=%async_computation.4 | async-start | bytes 524288 | tf_op jit(solution)/shard_map/all_to_all | solution.py:83
Sparse Core Ops, SparseCore 0:
  40.1 41.6 reduce-scatter.4
  84.4 38.1 reduce-scatter.6
  125.1 38.0 reduce-scatter.8
  165.6 37.8 reduce-scatter.10
